TPU v7x, 256 devices: a whole 4x4x8 slice. The times are simulated.
256 devices in a mesh: shard: 64 (over y, z_hi, x), rep: 4 (over z_lo, core).
Axes of the slice: x: 4, y: 4, z: 8 (z_hi: 4, z_lo: 2; z = z_hi * 2 + z_lo), core: 2. Of those that a mesh axis runs over, the one named last changes fastest.
Arguments:
- rows_in: bfloat16 [131072, 2048], P(('shard', 'rep')), may hold values from -24 to 24
- cotangent: bfloat16 [131072, 2048], P(('shard', 'rep')), may hold values from -24 to 24
- expert_counts: int32 [256, 2], P(('shard', 'rep')), may hold values from 0 to 512, as said below
- weights: bfloat16 [2048, 2, 1152], P('shard'), may hold values from -0.125 to 0.125
Outputs:
- rows_out: bfloat16 [131072, 2048], P(('shard', 'rep'))
- rows_grad: bfloat16 [131072, 2048], P(('shard', 'rep'))
- weight_grad: float32 [2048, 2, 1152], P('shard')
Inputs may be any that keep to these rules, and one draw needn't show every extreme that they name: `expert_counts`: on each device the experts' regions, each padded to a multiple of 128 rows, follow one another from row 0 and together fill at most 512 rows; some device fills all 512; one expert on some device holds all 512 rows.
All inputs are finite; a program needn't handle non-finite values.
Results may differ from a plain program's by a relative error of at most 0.0095.
Values may be sent and summed in bfloat16 or wider, within the bound.
No kernel may reach another device: no remote copies, remote signals or barrier semaphores. Data moves between devices by JAX's collectives and lax.ppermute only.
A program may use at most 128 MiB of HBM per device.

v0:
```python
import jax
import jax.numpy as jnp
from jax import lax
from jax.sharding import PartitionSpec as P

BLOCK = 128


def expert_block(inputs, upstream, expert_slab):
    hidden_width = expert_slab.shape[1] // 3
    gate_up = expert_slab[:, : 2 * hidden_width]
    down_t = expert_slab[:, 2 * hidden_width :]
    project = jnp.dot(inputs, gate_up, preferred_element_type=jnp.float32)
    gate_pre = project[:, :hidden_width]
    up_pre = project[:, hidden_width:]
    gate_sigmoid = jax.nn.sigmoid(gate_pre)
    active = gate_pre * gate_sigmoid
    hidden = (active * up_pre).astype(jnp.bfloat16)
    output = lax.dot_general(
        hidden, down_t, (((1,), (1,)), ((), ())), preferred_element_type=jnp.float32
    ).astype(jnp.bfloat16)
    hidden_grad = jnp.dot(upstream, down_t, preferred_element_type=jnp.float32)
    down_grad = lax.dot_general(
        upstream, hidden, (((0,), (0,)), ((), ())), preferred_element_type=jnp.float32
    )
    gate_grad = hidden_grad * up_pre * gate_sigmoid * (1.0 + gate_pre * (1.0 - gate_sigmoid))
    up_grad = hidden_grad * active
    joint_grad = jnp.concatenate([gate_grad, up_grad], axis=1).astype(jnp.bfloat16)
    proj_grad = lax.dot_general(
        inputs, joint_grad, (((0,), (0,)), ((), ())), preferred_element_type=jnp.float32
    )
    input_grad = lax.dot_general(
        joint_grad, gate_up, (((1,), (1,)), ((), ())), preferred_element_type=jnp.float32
    ).astype(jnp.bfloat16)
    return (output, input_grad, jnp.concatenate([proj_grad, down_grad], axis=1))


def alive_rows(counts, total_rows):
    padded = (counts + BLOCK - 1) // BLOCK * BLOCK
    starts = jnp.cumsum(padded) - padded
    position = jnp.arange(total_rows, dtype=jnp.int32)
    inside = (position[:, None] >= starts[None, :]) & (
        position[:, None] < (starts + counts)[None, :]
    )
    return (jnp.any(inside, axis=1), padded, starts)


def run_expert(expert_slab, inputs, upstream, start_row, nblocks, outputs, input_grads):

    def block_step(block_index, state):
        outputs, input_grads, grad_total = state
        row_begin = start_row + block_index * BLOCK
        block_in = lax.dynamic_slice_in_dim(inputs, row_begin, BLOCK, 0)
        block_up = lax.dynamic_slice_in_dim(upstream, row_begin, BLOCK, 0)
        output, input_grad, grad_piece = expert_block(block_in, block_up, expert_slab)
        outputs = lax.dynamic_update_slice_in_dim(outputs, output, row_begin, 0)
        input_grads = lax.dynamic_update_slice_in_dim(input_grads, input_grad, row_begin, 0)
        return (outputs, input_grads, grad_total + grad_piece)

    start_grad = jnp.zeros(expert_slab.shape, jnp.float32)
    return lax.fori_loop(jnp.int32(0), nblocks, block_step, (outputs, input_grads, start_grad))


def reduce_grads(grads):
    partial_sum = lax.psum_scatter(grads, "shard", scatter_dimension=0, tiled=True)
    return lax.psum(partial_sum.astype(jnp.bfloat16), "rep").astype(jnp.float32)


def local(rows_in, cotangent, expert_counts, weights):
    counts = expert_counts[0]
    alive, padded, starts = alive_rows(counts, rows_in.shape[0])
    inputs = jnp.where(alive[:, None], rows_in, jnp.zeros_like(rows_in))
    upstream = jnp.where(alive[:, None], cotangent, jnp.zeros_like(cotangent))
    outputs = jnp.zeros_like(rows_in)
    input_grads = jnp.zeros_like(rows_in)
    experts = weights.shape[1]
    pieces = []
    gathered = lax.all_gather(weights, "shard", axis=0, tiled=True)
    for expert in range(experts):
        outputs, input_grads, grad_total = run_expert(
            gathered[:, expert],
            inputs,
            upstream,
            starts[expert],
            padded[expert] // BLOCK,
            outputs,
            input_grads,
        )
        pieces.append(grad_total)
    reduced = reduce_grads(jnp.stack(pieces, axis=1))
    return (outputs, input_grads, reduced)


def solution(mesh):
    in_specs = (
        P(("shard", "rep"), None),
        P(("shard", "rep"), None),
        P(("shard", "rep"), None),
        P("shard", None, None),
    )
    out_specs = (P(("shard", "rep"), None), P(("shard", "rep"), None), P("shard", None, None))
    return jax.shard_map(local, mesh=mesh, in_specs=in_specs, out_specs=out_specs, check_vma=False)
```

profile of v0, /device:TPU:1, one launch (start us, length us, event | category | flops | bytes accessed | tf_op | source)
XLA Modules:
  0.0 623.0 jit_solution(16797978285030678725)
XLA Ops:
  7.2 1.6 copy.14
  17.0 4.0 broadcast_select_fusion
  21.0 109.1 %all-gather.2.cloned.1.call-done = bf16[2048,2,1152]{2,0,1:T(8,128)(2,1)} async-done(((bf16[32,2,1152]{2,0,1:T(8,128)(2,1)}), bf16[2048,2,1152]{2,0,1:T(8,128)(2,1)}) %all-gather.2.cloned.1.call-update) | async-done | bytes 9437200 | tf_op jit(solution)/shard_map/all_gather | solution.py:78
  130.1 8.2 %slice_bitcast_fusion = (bf16[2048,1152]{1,0:T(8,128)(2,1)}, bf16[2048,1152]{1,0:T(8,128)(2,1)}) fusion(bf16[2048,2,1152]{2,0,1:T(8,128)(2,1)} %all-gather.2.cloned.1.call-done), kind=kLoop, calls=%fused_computation.57 | loop fusion | bytes 18874368 | tf_op jit(solution)/shard_map/squeeze | solution.py:81
  138.3 1.6 broadcast.130.clone
  139.8 1.6 broadcast.130
  141.4 4.8 broadcast.131.clone
  146.2 24.7 %while.28 = (s32[]{:T(128)}, bf16[512,2048]{1,0:T(8,128)(2,1)}, bf16[512,2048]{1,0:T(8,128)(2,1)}, f32[2048,1152]{0,1:T(8,128)}, s32[]{:T(128)}, /*index=5*/s32[...) while((s32[]{:T(128)}, bf16[512,2048]{1,0:T(8,128)(2,1)}, ...), condition=%wide.region_3.4_spmd, body=%wide.region_2.3_spmd.sunk | while | flops 1818705920 | bytes 72974568 | solution.py:61
  146.9 2.6 fusion.87
  153.5 3.8 dynamic_update_slice.17
  157.3 3.8 dynamic_update_slice.16
  161.1 1.7 fusion.89
  163.8 7.1 %maximum_add_fusion.4 = f32[2048,1152]{0,1:T(8,128)} fusion(f32[2048,1152]{0,1:T(8,128)} %get-tuple-element.311, f32[2048,384]{0,1:T(8,128)S(1)} %fusion.89, f32[2048,768]{0,1:T(8,128)S(1)} %fusion.90), kind=kLoop, calls=%fused_computation.clone.1 | loop fusion | flops 4718592 | bytes 28311552 | tf_op jit(solution)/shard_map/while/body/add | solution.py:58
  170.9 9.6 %copy.15 = f32[2048,1152]{1,0:T(8,128)} copy(f32[2048,1152]{0,1:T(8,128)} %get-tuple-element.107) | data formatting | bytes 18874368 | tf_op jit(solution)/shard_map/while | solution.py:61
  180.5 4.8 broadcast.131
  185.4 49.4 %while.29 = (s32[]{:T(128)}, bf16[512,2048]{1,0:T(8,128)(2,1)}, bf16[512,2048]{1,0:T(8,128)(2,1)}, f32[2048,1152]{0,1:T(8,128)}, s32[]{:T(128)}, /*index=5*/s32[...) while((s32[]{:T(128)}, bf16[512,2048]{1,0:T(8,128)(2,1)}, ...), condition=%wide.region_5.6_spmd, body=%wide.region_4.5_spmd.sunk | while | flops 1818705920 | bytes 72974568 | solution.py:61
  186.0 2.6 fusion.99
  192.6 3.8 dynamic_update_slice.19
  196.4 3.8 dynamic_update_slice.18
  200.2 1.7 fusion.101
  202.9 7.1 %maximum_add_fusion.5 = f32[2048,1152]{0,1:T(8,128)} fusion(f32[2048,1152]{0,1:T(8,128)} %get-tuple-element.350, f32[2048,384]{0,1:T(8,128)S(1)} %fusion.101, f32[2048,768]{0,1:T(8,128)S(1)} %fusion.102), kind=kLoop, calls=%fused_computation.28.clone.1 | loop fusion | flops 4718592 | bytes 28311552 | tf_op jit(solution)/shard_map/while/body/add | solution.py:58
  210.7 2.6 fusion.99
  217.3 3.8 dynamic_update_slice.19
  221.1 3.8 dynamic_update_slice.18
  224.9 1.7 fusion.101
  227.6 7.1 %maximum_add_fusion.5 = f32[2048,1152]{0,1:T(8,128)} fusion(f32[2048,1152]{0,1:T(8,128)} %get-tuple-element.350, f32[2048,384]{0,1:T(8,128)S(1)} %fusion.101, f32[2048,768]{0,1:T(8,128)S(1)} %fusion.102), kind=kLoop, calls=%fused_computation.28.clone.1 | loop fusion | flops 4718592 | bytes 28311552 | tf_op jit(solution)/shard_map/while/body/add | solution.py:58
  234.7 9.7 %copy.16 = f32[2048,1152]{1,0:T(8,128)} copy(f32[2048,1152]{0,1:T(8,128)} %get-tuple-element.108) | data formatting | bytes 18874368 | tf_op jit(solution)/shard_map/while | solution.py:61
  244.5 14.5 %pad_maximum_fusion.6 = f32[2048,2,1152]{2,0,1:T(8,128)} fusion(f32[2048,1,1152]{2,0,1:T(8,128)} %bitcast.52, f32[2048,1,1152]{2,0,1:T(8,128)} %bitcast.51), kind=kLoop, calls=%fused_computation.56 | loop fusion | flops 4718592 | bytes 37748736 | tf_op jit(solution)/shard_map/stack | solution.py:90
  259.0 313.2 %reduce-scatter.2.cloned.1.call-done = f32[32,2,1152]{2,0,1:T(8,128)} async-done(((f32[2048,2,1152]{2,0,1:T(8,128)}), f32[32,2,1152]{2,0,1:T(8,128)}) %reduce-scatter.2.cloned.1.call-update) | async-done | bytes 294928 | tf_op jit(solution)/shard_map/reduce_scatter | solution.py:65
  572.2 1.6 convert_element_type.26
  573.9 40.8 %all-reduce.2.cloned.1.call-done = bf16[32,2,1152]{2,0,1:T(8,128)(2,1)} async-done(((bf16[32,2,1152]{2,0,1:T(8,128)(2,1)}), bf16[32,2,1152]{2,0,1:T(8,128)(2,1)}) %all-reduce.2.cloned.1.call-update) | async-done | bytes 147472 | tf_op jit(solution)/shard_map/psum | solution.py:66
  614.7 1.7 copy.17
  (30 shorter events, 17.9 us)
Async XLA Ops:
  7.2 122.9 %all-gather.2.cloned.1.call-start = ((), (), s32[]{:S(2)}) async-start(), calls=%async_computation.1 | async-start | bytes 9584640 | tf_op jit(solution)/shard_map/all_gather | solution.py:78
  8.8 563.4 %reduce-scatter.2.cloned.1.call-start = ((), (), s32[]{:S(2)}) async-start(), calls=%async_computation.2 | async-start | bytes 19169280 | tf_op jit(solution)/shard_map/reduce_scatter | solution.py:65
  146.9 3.3 copy-start.1
  186.0 3.3 copy-start
  210.7 3.3 copy-start
  259.0 355.8 %all-reduce.2.cloned.1.call-start = ((), (), s32[]{:S(2)}) async-start(), calls=%async_computation.3 | async-start | bytes 294912 | tf_op jit(solution)/shard_map/psum | solution.py:66
Sparse Core Ops, SparseCore 0:
  11.8 118.2 all-gather.1
  259.1 313.0 reduce-scatter.1
  575.6 39.0 all-reduce.1
where the time goes:
time: 624 us; the launch traced here: 623 us
  waiting for transfers between devices  463 us (74%)
  local copies, waits for them, and re-layouts  69 us (11%)
  other arithmetic  43.8 us (7%)
  matrix products  25.8 us (4%)
  between operations  19 us (3%)
    reduce_scatter x1, waiting for transfers between devices, reduce_grads(): lax.psum_scatter(grads, 'shard', scatter_dimension=0, tiled=True)  313 us
    all_gather x1, waiting for transfers between devices, local(): gathered = lax.all_gather(weights, 'shard', axis=0, tiled=True)  109 us
    psum x1, waiting for transfers between devices, reduce_grads(): return lax.psum(partial_sum.astype(jnp.bfloat16), 'rep').astype(jnp.float32)  40.8 us
    add x3, other arithmetic, block_step(): return (outputs, input_grads, grad_total + grad_piece)  21.4 us
    while x2, local copies, waits for them, and re-layouts, run_expert(): lax.fori_loop(jnp.int32(0), nblocks, block_step, (outputs, input_grads, s...  19.3 us
    another operation x1, other arithmetic, local(): reduced = reduce_grads(jnp.stack(pieces, axis=1))  14.5 us
    another operation x4, local copies, waits for them, and re-layouts  12.8 us
  transfers between devices with their start and end apart: 3, of which 3 were waited for; matrix products, arithmetic and copies ran while one was open for 1% of the time, Pallas kernels for 0%

commit v1 on v0

--- a/solution.py
+++ b/solution.py
@@ -4,6 +4,10 @@
 from jax.sharding import PartitionSpec as P
 
 BLOCK = 128
+
+
+def turn_point_by_axis(field_in, axis_name):
+    return jnp.sum(lax.all_gather(field_in, axis_name), 0)
 
 
 def expert_block(inputs, upstream, expert_slab):
@@ -63,7 +67,7 @@
 
 def reduce_grads(grads):
     partial_sum = lax.psum_scatter(grads, "shard", scatter_dimension=0, tiled=True)
-    return lax.psum(partial_sum.astype(jnp.bfloat16), "rep").astype(jnp.float32)
+    return turn_point_by_axis(partial_sum.astype(jnp.bfloat16), "rep").astype(jnp.float32)
 
 
 def local(rows_in, cotangent, expert_counts, weights):

time: 624 us -> 597 us (0.957)
  waiting for transfers between devices: 463 us -> 424 us
  blocking collectives: 0 us -> 8.07 us
    psum x1 -> x0, waiting for transfers between devices: 40.8 us -> none  [reduce_grads(): return lax.psum(partial_sum.astype(jnp.bfloat16), 'rep').astype(jnp.float32)]
    all_gather x0 -> x1, blocking collectives: none -> 8.07 us  [turn_point_by_axis(): return jnp.sum(lax.all_gather(field_in, axis_name), 0)]
  transfers between devices with their start and end apart: 3 -> 2, of which waited for: 3 -> 2; matrix products, arithmetic and copies ran while one was open for 1% -> 1% of each run, Pallas kernels for 0% -> 0%
where the time goes in v1:
time: 597 us; the launch traced here: 596 us
  waiting for transfers between devices  424 us (71%)
  local copies, waits for them, and re-layouts  68 us (11%)
  other arithmetic  42.8 us (7%)
  matrix products  31.5 us (5%)
  between operations  19.3 us (3%)
  blocking collectives  8.07 us (1%)
    reduce_scatter x1, waiting for transfers between devices, reduce_grads(): lax.psum_scatter(grads, 'shard', scatter_dimension=0, tiled=True)  315 us
    all_gather x1, waiting for transfers between devices, local(): gathered = lax.all_gather(weights, 'shard', axis=0, tiled=True)  109 us
    add x3, other arithmetic, block_step(): return (outputs, input_grads, grad_total + grad_piece)  21 us
    while x2, local copies, waits for them, and re-layouts, run_expert(): lax.fori_loop(jnp.int32(0), nblocks, block_step, (outputs, input_grads, s...  19.3 us
    another operation x1, other arithmetic, local(): reduced = reduce_grads(jnp.stack(pieces, axis=1))  14.4 us
    another operation x4, local copies, waits for them, and re-layouts  12.8 us
  transfers between devices with their start and end apart: 2, of which 2 were waited for; matrix products, arithmetic and copies ran while one was open for 1% of the time, Pallas kernels for 0%

profile of v1, /device:TPU:1, one launch (start us, length us, event | category | flops | bytes accessed | tf_op | source)
XLA Modules:
  0.0 595.9 jit_solution(16863539288652338063)
XLA Ops:
  7.2 1.6 copy.15
  17.0 4.0 broadcast_select_fusion
  20.9 109.2 %all-gather.3.cloned.1.call-done = bf16[2048,2,1152]{2,0,1:T(8,128)(2,1)} async-done(((bf16[32,2,1152]{2,0,1:T(8,128)(2,1)}), bf16[2048,2,1152]{2,0,1:T(8,128)(2,1)}) %all-gather.3.cloned.1.call-update) | async-done | bytes 9437200 | tf_op jit(solution)/shard_map/all_gather | solution.py:82
  130.1 8.1 %slice_bitcast_fusion = (bf16[2048,1152]{1,0:T(8,128)(2,1)}, bf16[2048,1152]{1,0:T(8,128)(2,1)}) fusion(bf16[2048,2,1152]{2,0,1:T(8,128)(2,1)} %all-gather.3.cloned.1.call-done), kind=kLoop, calls=%fused_computation.57 | loop fusion | bytes 18874368 | tf_op jit(solution)/shard_map/squeeze | solution.py:85
  138.2 1.6 broadcast.130
  141.4 4.8 broadcast.131.clone
  146.2 26.4 %while.28 = (s32[]{:T(128)}, bf16[512,2048]{1,0:T(8,128)(2,1)}, bf16[512,2048]{1,0:T(8,128)(2,1)}, f32[2048,1152]{0,1:T(8,128)}, s32[]{:T(128)}, /*index=5*/s32[...) while((s32[]{:T(128)}, bf16[512,2048]{1,0:T(8,128)(2,1)}, ...), condition=%wide.region_3.4_spmd, body=%wide.region_2.3_spmd.sunk | while | flops 1818705920 | bytes 72974576 | solution.py:65
  146.8 2.6 fusion.87
  152.3 3.8 dynamic_update_slice.16
  156.1 3.0 fusion.88
  159.1 3.8 dynamic_update_slice.17
  162.9 1.7 fusion.89
  165.6 7.0 %maximum_add_fusion.4 = f32[2048,1152]{0,1:T(8,128)} fusion(f32[2048,1152]{0,1:T(8,128)} %get-tuple-element.311, f32[2048,384]{0,1:T(8,128)S(1)} %fusion.89, f32[2048,768]{0,1:T(8,128)S(1)} %fusion.90), kind=kLoop, calls=%fused_computation.clone.1 | loop fusion | flops 4718592 | bytes 28311552 | tf_op jit(solution)/shard_map/while/body/add | solution.py:62
  172.6 4.8 broadcast.131
  177.5 52.9 %while.29 = (s32[]{:T(128)}, bf16[512,2048]{1,0:T(8,128)(2,1)}, bf16[512,2048]{1,0:T(8,128)(2,1)}, f32[2048,1152]{0,1:T(8,128)}, s32[]{:T(128)}, /*index=5*/s32[...) while((s32[]{:T(128)}, bf16[512,2048]{1,0:T(8,128)(2,1)}, ...), condition=%wide.region_5.6_spmd, body=%wide.region_4.5_spmd.sunk | while | flops 1818705920 | bytes 72974576 | solution.py:65
  178.1 2.6 fusion.99
  183.5 3.8 dynamic_update_slice.18
  187.3 3.0 fusion.100
  190.4 3.8 dynamic_update_slice.19
  194.2 1.7 fusion.101
  196.9 7.0 %maximum_add_fusion.5 = f32[2048,1152]{0,1:T(8,128)} fusion(f32[2048,1152]{0,1:T(8,128)} %get-tuple-element.350, f32[2048,384]{0,1:T(8,128)S(1)} %fusion.101, f32[2048,768]{0,1:T(8,128)S(1)} %fusion.102), kind=kLoop, calls=%fused_computation.28.clone.1 | loop fusion | flops 4718592 | bytes 28311552 | tf_op jit(solution)/shard_map/while/body/add | solution.py:62
  204.6 2.6 fusion.99
  210.0 3.8 dynamic_update_slice.18
  213.8 3.0 fusion.100
  216.8 3.8 dynamic_update_slice.19
  220.6 1.7 fusion.101
  223.3 7.0 %maximum_add_fusion.5 = f32[2048,1152]{0,1:T(8,128)} fusion(f32[2048,1152]{0,1:T(8,128)} %get-tuple-element.350, f32[2048,384]{0,1:T(8,128)S(1)} %fusion.101, f32[2048,768]{0,1:T(8,128)S(1)} %fusion.102), kind=kLoop, calls=%fused_computation.28.clone.1 | loop fusion | flops 4718592 | bytes 28311552 | tf_op jit(solution)/shard_map/while/body/add | solution.py:62
  230.3 9.7 %copy.17 = f32[2048,1152]{1,0:T(8,128)} copy(f32[2048,1152]{0,1:T(8,128)} %get-tuple-element.108) | data formatting | bytes 18874368 | tf_op jit(solution)/shard_map/while | solution.py:65
  240.0 9.6 %copy.16 = f32[2048,1152]{1,0:T(8,128)} copy(f32[2048,1152]{0,1:T(8,128)} %get-tuple-element.107) | data formatting | bytes 18874368 | tf_op jit(solution)/shard_map/while | solution.py:65
  249.6 14.4 %pad_maximum_fusion.6 = f32[2048,2,1152]{2,0,1:T(8,128)} fusion(f32[2048,1,1152]{2,0,1:T(8,128)} %bitcast.52, f32[2048,1,1152]{2,0,1:T(8,128)} %bitcast.53), kind=kLoop, calls=%fused_computation.56 | loop fusion | flops 4718592 | bytes 37748736 | tf_op jit(solution)/shard_map/stack | solution.py:94
  264.1 314.9 %reduce-scatter.2.cloned.1.call-done = f32[32,2,1152]{2,0,1:T(8,128)} async-done(((f32[2048,2,1152]{2,0,1:T(8,128)}), f32[32,2,1152]{2,0,1:T(8,128)}) %reduce-scatter.2.cloned.1.call-update) | async-done | bytes 294928 | tf_op jit(solution)/shard_map/reduce_scatter | solution.py:69
  580.0 8.1 %all-gather = bf16[128,2,1152]{2,0,1:T(8,128)(2,1)S(1)} all-gather(bf16[32,2,1152]{2,0,1:T(8,128)(2,1)S(1)} %convert_element_type.28), channel_id=2, replica_groups=mesh['shard'=64,'rep'=4] {'rep'}, dimensions={0}, use_global_device_ids=true | all-gather | bytes 737280 | tf_op jit(solution)/shard_map/all_gather | solution.py:10
  (29 shorter events, 17.8 us)
Async XLA Ops:
  7.2 122.9 %all-gather.3.cloned.1.call-start = ((), (), s32[]{:S(2)}) async-start(), calls=%async_computation.1 | async-start | bytes 9584640 | tf_op jit(solution)/shard_map/all_gather | solution.py:82
  8.8 570.2 %reduce-scatter.2.cloned.1.call-start = ((), (), s32[]{:S(2)}) async-start(), calls=%async_computation.2 | async-start | bytes 19169280 | tf_op jit(solution)/shard_map/reduce_scatter | solution.py:69
  146.8 3.3 copy-start.1
  178.1 3.3 copy-start
  204.5 3.3 copy-start
Sparse Core Ops, SparseCore 0:
  11.8 118.2 all-gather.2
  264.2 314.7 reduce-scatter.1
